TPU v7x, 256 devices: a whole 4x4x8 slice. The times are simulated.
256 devices in a mesh: segment: 4 (over x), dp: 64 (over z, y, core).
Axes of the slice: x: 4, y: 4, z: 8, core: 2. Of those that a mesh axis runs over, the one named last changes fastest.
Arguments:
- x_saved: bfloat16 [4, 8192, 1536], P('segment', 'dp'), may hold values from -6 to 6
- gains: float32 [4, 1536], P('segment'), may hold values from 0.1 to 1.9
- w_in: bfloat16 [4, 1536, 3072], P('segment', 'dp'), may hold values from -0.15625 to 0.15625
- w_out: bfloat16 [4, 3072, 1536], P('segment', None, 'dp'), may hold values from -0.109375 to 0.109375
- cotangent: bfloat16 [8192, 1536], P('dp'), may hold values from -6 to 6
- lengths: int32 [64], replicated, may hold values from 1 to 256, 8192 in all
Outputs:
- grads: bfloat16 [4, 8192, 1536], P('segment', 'dp')
- gain_grads: float32 [4, 1536], P('segment')
All inputs are finite; a program needn't handle non-finite values.
Results may differ from a plain program's by a relative error of at most 0.0075.
Values may be sent and summed in bfloat16 or wider, within the bound.
No kernel may reach another device: no remote copies, remote signals or barrier semaphores. Data moves between devices by JAX's collectives and lax.ppermute only.
A program may use at most 128 MiB of HBM per device.

v0:
```python
import jax
import jax.numpy as jnp
from jax import lax
from jax.sharding import PartitionSpec as P


def passed_along(x, axis, by):
    length = lax.axis_size(axis)
    pairs = [(i, i + by) for i in range(length) if 0 <= i + by < length]
    return lax.ppermute(x, axis, pairs)


def on_device(x_saved, gains, w_in, w_out, cotangent, lengths):
    rows = cotangent.shape[0]
    width = cotangent.shape[1]
    ends = jnp.cumsum(lengths)
    position = lax.axis_index("dp") * rows + jnp.arange(rows, dtype=jnp.int32)
    utter_hit = (position[:, None] >= ends[None, :]).astype(jnp.int32)
    utter = jnp.sum(utter_hit, 1)
    onehot = (utter[:, None] == jnp.arange(lengths.shape[0], dtype=jnp.int32)[None, :]).astype(
        jnp.int32
    )
    tok_len = jnp.sum(onehot * lengths[None, :], 1).astype(jnp.float32)
    weight = 2.0 * rows / (tok_len + rows)
    current = (cotangent.astype(jnp.float32) * weight[:, None]).astype(jnp.bfloat16)
    xf = x_saved[0].astype(jnp.float32)
    centered_input = xf - jnp.mean(xf, -1, keepdims=True)
    variance = jnp.mean(centered_input * centered_input, -1, keepdims=True)
    inverse_deviation = lax.rsqrt(variance + 1e-05)
    standardized_input = centered_input * inverse_deviation
    gain_vector = gains[0]
    normalized_input = (standardized_input * gain_vector).astype(jnp.bfloat16)
    w_first, w_second = (
        lax.all_gather(w_in[0], "dp", axis=0, tiled=True),
        lax.all_gather(w_out[0], "dp", axis=1, tiled=True),
    )

    def project_all(normed_rows, grad_in):
        hidden = jnp.dot(normed_rows, w_first, preferred_element_type=jnp.float32)
        up_grad = jnp.dot(grad_in, w_second.T, preferred_element_type=jnp.float32)
        sig = jax.nn.sigmoid(hidden)
        hid_grad = (0.5 * up_grad * (sig + hidden * sig * (1.0 - sig))).astype(jnp.bfloat16)
        return jnp.dot(hid_grad, w_first.T, preferred_element_type=jnp.float32)

    def block_back():

        def run(grad_in):
            norm_gradient = project_all(normalized_input, grad_in)
            gain_partial = jnp.sum(norm_gradient * standardized_input, 0)
            gain_scaled = norm_gradient * gain_vector
            backward_result = inverse_deviation * (
                gain_scaled
                - jnp.mean(gain_scaled, -1, keepdims=True)
                - standardized_input * jnp.mean(gain_scaled * standardized_input, -1, keepdims=True)
            )
            return (
                (grad_in.astype(jnp.float32) + backward_result).astype(jnp.bfloat16),
                gain_partial,
            )

        return run

    def pass_through(grad_in):
        return (grad_in, jnp.zeros((width,), jnp.float32))

    segments = lax.axis_size("segment")
    my_segment = lax.axis_index("segment")
    gain_local = jnp.zeros((width,), jnp.float32)
    result = current
    for level in range(segments - 1, -1, -1):
        mine = my_segment == level
        updated, gain_partial = lax.cond(mine, block_back(), pass_through, current)
        result = jnp.where(mine, updated, result)
        gain_local = jnp.where(mine, gain_partial, gain_local)
        if level > 0:
            current = passed_along(updated, "segment", -1)
    gain_total = lax.psum(gain_local, "dp")
    return (result[None], gain_total[None])


def solution(mesh):
    in_specs = (
        P("segment", "dp", None),
        P("segment", None),
        P("segment", "dp", None),
        P("segment", None, "dp"),
        P("dp", None),
        P(),
    )
    out_specs = (P("segment", "dp", None), P("segment", None))
    return jax.shard_map(
        on_device, mesh=mesh, in_specs=in_specs, out_specs=out_specs, check_vma=False
    )
```

profile of v0, /device:TPU:1, one launch (start us, length us, event | category | flops | bytes accessed | tf_op | source)
XLA Modules:
  0.0 432.3 jit_solution(9842427514506412659)
XLA Ops:
  7.2 0.0 all-gather.7.cloned.1.call-start
  7.2 0.7 all-gather.7.cloned.1.call-update
  7.9 0.0 all-gather.5.cloned.1.call-start
  7.9 0.7 all-gather.5.cloned.1.call-update
  8.7 0.7 copy.17
  9.4 0.1 reduce-window.8
  9.5 0.1 reduce.5
  9.6 0.7 reduce.6
  10.3 0.1 convert_reduce_fusion.1
  10.4 0.7 select_reduce_fusion
  11.2 0.0 copy-start
  11.2 1.1 convert_reduce_fusion
  12.3 1.2 fusion.23
  13.6 0.0 copy-start.4
  13.6 1.5 fusion.21
  15.1 84.0 %all-gather.7.cloned.1.call-done = bf16[1,1536,3072]{2,1,0:T(8,128)(2,1)} async-done(((bf16[1,24,3072]{2,1,0:T(8,128)(2,1)}), bf16[1,1536,3072]{2,1,0:T(8,128)(2,1)}) %all-gather.7.cloned.1.call-update) | async-done | bytes 9437200 | tf_op jit(solution)/shard_map/all_gather | solution.py:34
  99.1 84.1 %all-gather.5.cloned.1.call-done = bf16[1,3072,1536]{1,2,0:T(8,128)(2,1)} async-done(((bf16[1,3072,24]{1,2,0:T(8,128)(2,1)}), bf16[1,3072,1536]{1,2,0:T(8,128)(2,1)}) %all-gather.5.cloned.1.call-update) | async-done | bytes 9437200 | tf_op jit(solution)/shard_map/all_gather | solution.py:35
  183.2 0.0 copy-done
  183.2 0.0 copy-done.4
  183.2 0.6 conditional.4
  183.3 0.6 broadcast.129
  183.9 1.3 collective-permute-start
  185.1 11.0 %collective-permute-done = bf16[128,1536]{1,0:T(8,128)(2,1)S(1)} collective-permute-done((bf16[128,1536]{1,0:T(8,128)(2,1)S(1)}, bf16[128,1536]{1,0:T(8,128)(2,1)S(1)}, u32[]{:S(2)}, u32[]{:S(2)}) %collective-permute-start) | collective-permute-done | bytes 393248 | tf_op jit(solution)/shard_map/ppermute | solution.py:10
  196.2 0.0 copy-start.2
  196.2 1.3 collective-permute-start.1
  197.4 10.1 %collective-permute-done.1 = bf16[128,1536]{1,0:T(8,128)(2,1)S(1)} collective-permute-done((bf16[128,1536]{1,0:T(8,128)(2,1)S(1)}, bf16[128,1536]{1,0:T(8,128)(2,1)S(1)}, u32[]{:S(2)}, u32[]{:S(2)}) %collective-permute-start.1) | collective-permute-done | bytes 393248 | tf_op jit(solution)/shard_map/ppermute | solution.py:10
  207.6 0.0 copy-done.2
  207.6 0.6 conditional.6
  207.6 0.6 broadcast.137
  208.2 1.3 collective-permute-start.2
  209.5 66.8 %collective-permute-done.2 = bf16[128,1536]{1,0:T(8,128)(2,1)S(1)} collective-permute-done((bf16[128,1536]{1,0:T(8,128)(2,1)S(1)}, bf16[128,1536]{1,0:T(8,128)(2,1)S(1)}, u32[]{:S(2)}, u32[]{:S(2)}) %collective-permute-start.2) | collective-permute-done | bytes 393248 | tf_op jit(solution)/shard_map/ppermute | solution.py:10
  276.3 0.0 copy-start.1
  276.3 0.0 copy-start.3
  276.3 20.4 %conditional.7 = (bf16[128,1536]{1,0:T(8,128)(2,1)S(1)}, f32[1536]{0:T(1024)S(1)}) conditional(s32[]{:T(128)} %convert_element_type.77, bf16[128,1536]{1,0:T(8,128)(2,1)S(1)} %collective-permute-done.2, (bf16[128,1536]{1,0:T(8,128)(2,1)S(1)}, f32[128,1]{0,1:T(1,128)}, bf16[3072,1536]{0,1:T(8,128)(2,1)}, bf16[128,1536]{1,0:T(8,128)(2,1)S(1)}, ...), branch_computations={%region_20.21_spmd, %region_21.25_spmd} | conditional | flops 3630562048 | bytes 36213296 | solution.py:72
  276.3 6.2 %fusion.28 = f32[128,3072]{1,0:T(8,128)} fusion(bf16[128,1536]{1,0:T(8,128)(2,1)S(1)} %get-tuple-element.84, bf16[1536,3072]{1,0:T(8,128)(2,1)} %get-tuple-element.85), kind=kOutput, calls=%fused_computation.69 | convolution fusion | flops 1207959552 | bytes 11403264 | tf_op jit(solution)/shard_map/cond/branch_1_fun/dot_general | solution.py:39
  282.5 0.0 copy-start.7
  282.5 12.7 %multiply_reduce_fusion.9 = (f32[1536]{0:T(1024)S(1)}, f32[128]{0:T(128)S(1)}, f32[128]{0:T(128)S(1)}, f32[128,1536]{1,0:T(8,128)}) fusion(f32[128,1536]{1,0:T(8,128)S(1)} %get-tuple-element.87, f32[1536]{0:T(1024)S(1)} %reduce.4, bf16[1536,3072]{1,0:T(8,128)(2,1)} %get-tuple-element.85, bf16[128,1536]{1,0:T(8,128)(2,1)S(1)} %get-tuple-element.81, ...), kind=kOutput, calls=%fused_computation.39 | convolution fusion | flops 2421029376 | bytes 22426624 | tf_op jit(solution)/shard_map/cond/branch_1_fun/dot_general | solution.py:43
  295.2 0.0 copy-done.7
  295.2 1.4 add_convert_fusion.3
  296.7 0.0 copy-done.1
  296.7 0.0 copy-done.3
  296.7 0.8 select_bitcast_fusion
  297.5 128.0 %psum.7 = f32[1,1536]{1,0:T(1,128)} all-reduce(f32[1,1536]{1,0:T(1,128)S(1)} %broadcast_in_dim.5), channel_id=1, replica_groups=mesh['segment'=4,'dp'=64] {'dp'}, use_global_device_ids=true, to_apply=%region_25.26 | all-reduce | flops 1536 | bytes 12288 | tf_op jit(solution)/shard_map/psum | solution.py:77
  (11 shorter events, 0.1 us)
Async XLA Ops:
  7.2 92.0 %all-gather.7.cloned.1.call-start = ((), (), s32[]{:S(2)}) async-start(), calls=%async_computation.1 | async-start | bytes 9584640 | tf_op jit(solution)/shard_map/all_gather | solution.py:34
  7.9 175.3 %all-gather.5.cloned.1.call-start = ((), (), s32[]{:S(2)}) async-start(), calls=%async_computation | async-start | bytes 9584640 | tf_op jit(solution)/shard_map/all_gather | solution.py:35
  11.2 172.0 %copy-start = (f32[1,1536]{1,0:T(1,128)S(1)}, f32[1,1536]{1,0:T(1,128)}, u32[]{:S(2)}) copy-start(f32[1,1536]{1,0:T(1,128)} %param.15) | copy-start | bytes 18436
  13.6 169.6 %copy-start.4 = (f32[128,1]{0,1:T(1,128)}, f32[128,1]{0,1:T(1,128)S(1)}, u32[]{:S(2)}) copy-start(f32[128,1]{0,1:T(1,128)S(1)} %get-tuple-element.189) | copy-start | bytes 1540
  183.9 12.3 %collective-permute-start = (bf16[128,1536]{1,0:T(8,128)(2,1)S(1)}, bf16[128,1536]{1,0:T(8,128)(2,1)S(1)}, u32[]{:S(2)}, u32[]{:S(2)}) collective-permute-start(bf16[128,1536]{1,0:T(8,128)(2,1)S(1)} %get-tuple-element.98), channel_id=1, source_target_pairs={{64,0},{128,64},{192,128},{65,1},{129,65},{193,129},{66,2},{130,66... | collective-permute-start | bytes 1179656 | tf_op jit(solution)/shard_map/ppermute | solution.py:10
  196.2 11.4 %copy-start.2 = (f32[1536]{0:T(1024)}, f32[1536]{0:T(1024)S(1)}, u32[]{:S(2)}) copy-start(f32[1536]{0:T(1024)S(1)} %get-tuple-element.104) | copy-start | bytes 18436
  196.2 11.4 %collective-permute-start.1 = (bf16[128,1536]{1,0:T(8,128)(2,1)S(1)}, bf16[128,1536]{1,0:T(8,128)(2,1)S(1)}, u32[]{:S(2)}, u32[]{:S(2)}) collective-permute-start(bf16[128,1536]{1,0:T(8,128)(2,1)S(1)} %get-tuple-element.99), channel_id=1, source_target_pairs={{64,0},{128,64},{192,128},{65,1},{129,65},{193,129},{66,2},{130,66... | collective-permute-start | bytes 1179656 | tf_op jit(solution)/shard_map/ppermute | solution.py:10
  208.2 68.1 %collective-permute-start.2 = (bf16[128,1536]{1,0:T(8,128)(2,1)S(1)}, bf16[128,1536]{1,0:T(8,128)(2,1)S(1)}, u32[]{:S(2)}, u32[]{:S(2)}) collective-permute-start(bf16[128,1536]{1,0:T(8,128)(2,1)S(1)} %get-tuple-element.100), channel_id=1, source_target_pairs={{64,0},{128,64},{192,128},{65,1},{129,65},{193,129},{66,2},{130,66... | collective-permute-start | bytes 1179656 | tf_op jit(solution)/shard_map/ppermute | solution.py:10
  276.3 20.4 %copy-start.1 = (f32[1536]{0:T(1024)S(1)}, f32[1536]{0:T(1024)}, u32[]{:S(2)}) copy-start(f32[1536]{0:T(1024)} %get-tuple-element.105) | copy-start | bytes 18436
  276.3 20.4 %copy-start.3 = (f32[1536]{0:T(1024)S(1)}, f32[1536]{0:T(1024)}, u32[]{:S(2)}) copy-start(f32[1536]{0:T(1024)} %copy-done.2) | copy-start | bytes 18436
  282.5 12.7 %copy-start.7 = (f32[128,1]{0,1:T(1,128)S(1)}, f32[128,1]{0,1:T(1,128)}, u32[]{:S(2)}) copy-start(f32[128,1]{0,1:T(1,128)} %get-tuple-element.82) | copy-start | bytes 1540 | tf_op jit(solution)/shard_map/cond
Sparse Core Ops, SparseCore 0:
  10.7 88.3 all-gather.6
  101.8 81.3 all-gather.4
where the time goes:
time: 433 us; the launch traced here: 432 us
  waiting for transfers between devices  257 us (59%)
  blocking collectives  128 us (30%)
  matrix products  18.9 us (4%)
  between operations  14.2 us (3%)
  other arithmetic  7.95 us (2%)
    psum x1, blocking collectives, on_device(): gain_total = lax.psum(gain_local, 'dp')  128 us
    ppermute x3, waiting for transfers between devices, passed_along(): return lax.ppermute(x, axis, pairs)  87.9 us
    all_gather x1, waiting for transfers between devices, on_device(): lax.all_gather(w_out[0], 'dp', axis=1, tiled=True)  84.1 us
    all_gather x1, waiting for transfers between devices, on_device(): lax.all_gather(w_in[0], 'dp', axis=0, tiled=True)  84 us
    dot_general x1, matrix products, project_all(): return jnp.dot(hid_grad, w_first.T, preferred_element_type=jnp.float32)  12.7 us
  transfers between devices with their start and end apart: 5, of which 5 were waited for; matrix products, arithmetic and copies ran while one was open for 1% of the time, Pallas kernels for 0%

commit v1 on v0

--- a/solution.py
+++ b/solution.py
@@ -74,7 +74,8 @@
         gain_local = jnp.where(mine, gain_partial, gain_local)
         if level > 0:
             current = passed_along(updated, "segment", -1)
-    gain_total = lax.psum(gain_local, "dp")
+    pieces = lax.all_gather(gain_local, "dp")
+    gain_total = jnp.sum(pieces, axis=0)
     return (result[None], gain_total[None])
 
 

time: 433 us -> 355 us (0.82)
  blocking collectives: 128 us -> 49.4 us
    psum x1 -> x0, blocking collectives: 128 us -> none  [on_device(): gain_total = lax.psum(gain_local, 'dp')]
    all_gather x0 -> x1, blocking collectives: none -> 49.4 us  [on_device(): pieces = lax.all_gather(gain_local, 'dp')]
  transfers between devices with their start and end apart: 5 -> 5, of which waited for: 5 -> 5; matrix products, arithmetic and copies ran while one was open for 1% -> 2% of each run, Pallas kernels for 0% -> 0%
where the time goes in v1:
time: 355 us
  waiting for transfers between devices  257 us (72%)
  blocking collectives  49.4 us (14%)
  matrix products  18.9 us (5%)
  between operations  14.2 us (4%)
  other arithmetic  8.2 us (2%)
  starting transfers between devices  3.92 us (1%)
    ppermute x3, waiting for transfers between devices, passed_along(): return lax.ppermute(x, axis, pairs)  87.9 us
    all_gather x1, waiting for transfers between devices, on_device(): lax.all_gather(w_out[0], 'dp', axis=1, tiled=True)  84.1 us
    all_gather x1, waiting for transfers between devices, on_device(): lax.all_gather(w_in[0], 'dp', axis=0, tiled=True)  84 us
    all_gather x1, blocking collectives, on_device(): pieces = lax.all_gather(gain_local, 'dp')  49.4 us
    dot_general x1, matrix products, project_all(): return jnp.dot(hid_grad, w_first.T, preferred_element_type=jnp.float32)  12.7 us
  transfers between devices with their start and end apart: 5, of which 5 were waited for; matrix products, arithmetic and copies ran while one was open for 2% of the time, Pallas kernels for 0%

profile of v1, /device:TPU:1, one launch (start us, length us, event | category | flops | bytes accessed | tf_op | source)
XLA Modules:
  0.0 354.6 jit_solution(9302220753078983392)
XLA Ops:
  7.2 0.0 all-gather.9.cloned.1.call-start
  7.2 0.7 all-gather.9.cloned.1.call-update
  7.9 0.0 all-gather.7.cloned.1.call-start
  7.9 0.7 all-gather.7.cloned.1.call-update
  8.7 0.7 copy.17
  9.4 0.1 reduce-window.8
  9.5 0.1 reduce.6
  9.6 0.7 reduce.7
  10.3 0.1 convert_reduce_fusion.1
  10.4 0.7 select_reduce_fusion
  11.2 0.0 copy-start
  11.2 1.1 convert_reduce_fusion
  12.3 1.2 fusion.23
  13.6 0.0 copy-start.4
  13.6 1.5 fusion.21
  15.1 84.0 %all-gather.9.cloned.1.call-done = bf16[1,1536,3072]{2,1,0:T(8,128)(2,1)} async-done(((bf16[1,24,3072]{2,1,0:T(8,128)(2,1)}), bf16[1,1536,3072]{2,1,0:T(8,128)(2,1)}) %all-gather.9.cloned.1.call-update) | async-done | bytes 9437200 | tf_op jit(solution)/shard_map/all_gather | solution.py:34
  99.1 84.1 %all-gather.7.cloned.1.call-done = bf16[1,3072,1536]{1,2,0:T(8,128)(2,1)} async-done(((bf16[1,3072,24]{1,2,0:T(8,128)(2,1)}), bf16[1,3072,1536]{1,2,0:T(8,128)(2,1)}) %all-gather.7.cloned.1.call-update) | async-done | bytes 9437200 | tf_op jit(solution)/shard_map/all_gather | solution.py:35
  183.2 0.0 copy-done
  183.2 0.0 copy-done.4
  183.2 0.6 conditional.4
  183.3 0.6 broadcast.129
  183.9 1.3 collective-permute-start
  185.1 11.0 %collective-permute-done = bf16[128,1536]{1,0:T(8,128)(2,1)S(1)} collective-permute-done((bf16[128,1536]{1,0:T(8,128)(2,1)S(1)}, bf16[128,1536]{1,0:T(8,128)(2,1)S(1)}, u32[]{:S(2)}, u32[]{:S(2)}) %collective-permute-start) | collective-permute-done | bytes 393248 | tf_op jit(solution)/shard_map/ppermute | solution.py:10
  196.2 0.0 copy-start.2
  196.2 1.3 collective-permute-start.1
  197.4 10.1 %collective-permute-done.1 = bf16[128,1536]{1,0:T(8,128)(2,1)S(1)} collective-permute-done((bf16[128,1536]{1,0:T(8,128)(2,1)S(1)}, bf16[128,1536]{1,0:T(8,128)(2,1)S(1)}, u32[]{:S(2)}, u32[]{:S(2)}) %collective-permute-start.1) | collective-permute-done | bytes 393248 | tf_op jit(solution)/shard_map/ppermute | solution.py:10
  207.6 0.0 copy-done.2
  207.6 0.6 conditional.6
  207.6 0.6 broadcast.137
  208.2 1.3 collective-permute-start.2
  209.5 66.8 %collective-permute-done.2 = bf16[128,1536]{1,0:T(8,128)(2,1)S(1)} collective-permute-done((bf16[128,1536]{1,0:T(8,128)(2,1)S(1)}, bf16[128,1536]{1,0:T(8,128)(2,1)S(1)}, u32[]{:S(2)}, u32[]{:S(2)}) %collective-permute-start.2) | collective-permute-done | bytes 393248 | tf_op jit(solution)/shard_map/ppermute | solution.py:10
  276.3 0.0 copy-start.1
  276.3 0.0 copy-start.3
  276.3 20.4 %conditional.7 = (bf16[128,1536]{1,0:T(8,128)(2,1)S(1)}, f32[1536]{0:T(1024)S(1)}) conditional(s32[]{:T(128)} %convert_element_type.77, bf16[128,1536]{1,0:T(8,128)(2,1)S(1)} %collective-permute-done.2, (bf16[128,1536]{1,0:T(8,128)(2,1)S(1)}, f32[128,1]{0,1:T(1,128)}, bf16[3072,1536]{0,1:T(8,128)(2,1)}, bf16[128,1536]{1,0:T(8,128)(2,1)S(1)}, ...), branch_computations={%region_20.21_spmd, %region_21.25_spmd} | conditional | flops 3630562048 | bytes 36213296 | solution.py:72
  276.3 6.2 %fusion.28 = f32[128,3072]{1,0:T(8,128)} fusion(bf16[128,1536]{1,0:T(8,128)(2,1)S(1)} %get-tuple-element.84, bf16[1536,3072]{1,0:T(8,128)(2,1)} %get-tuple-element.85), kind=kOutput, calls=%fused_computation.69 | convolution fusion | flops 1207959552 | bytes 11403264 | tf_op jit(solution)/shard_map/cond/branch_1_fun/dot_general | solution.py:39
  282.5 0.0 copy-start.7
  282.5 12.7 %multiply_reduce_fusion.9 = (f32[1536]{0:T(1024)S(1)}, f32[128]{0:T(128)S(1)}, f32[128]{0:T(128)S(1)}, f32[128,1536]{1,0:T(8,128)}) fusion(f32[128,1536]{1,0:T(8,128)S(1)} %get-tuple-element.87, f32[1536]{0:T(1024)S(1)} %reduce.5, bf16[1536,3072]{1,0:T(8,128)(2,1)} %get-tuple-element.85, bf16[128,1536]{1,0:T(8,128)(2,1)S(1)} %get-tuple-element.81, ...), kind=kOutput, calls=%fused_computation.39 | convolution fusion | flops 2421029376 | bytes 22426624 | tf_op jit(solution)/shard_map/cond/branch_1_fun/dot_general | solution.py:43
  295.2 0.0 copy-done.7
  295.2 1.4 add_convert_fusion.3
  296.7 0.0 copy-done.1
  296.7 0.0 copy-done.3
  296.7 0.8 select_bitcast_fusion
  297.5 49.4 %all-gather.3 = f32[64,1,1536]{2,1,0:T(1,128)S(1)} all-gather(f32[1,1,1536]{2,1,0:T(1,128)S(1)} %reshape.102), channel_id=4, replica_groups=mesh['segment'=4,'dp'=64] {'dp'}, dimensions={0}, use_global_device_ids=true | all-gather | bytes 399360 | tf_op jit(solution)/shard_map/all_gather | solution.py:77
  346.9 0.2 reduce_sum.157
  347.2 0.6 broadcast_in_dim.5
  (11 shorter events, 0.1 us)
Async XLA Ops:
  7.2 92.0 %all-gather.9.cloned.1.call-start = ((), (), s32[]{:S(2)}) async-start(), calls=%async_computation.1 | async-start | bytes 9584640 | tf_op jit(solution)/shard_map/all_gather | solution.py:34
  7.9 175.3 %all-gather.7.cloned.1.call-start = ((), (), s32[]{:S(2)}) async-start(), calls=%async_computation | async-start | bytes 9584640 | tf_op jit(solution)/shard_map/all_gather | solution.py:35
  11.2 172.0 %copy-start = (f32[1,1536]{1,0:T(1,128)S(1)}, f32[1,1536]{1,0:T(1,128)}, u32[]{:S(2)}) copy-start(f32[1,1536]{1,0:T(1,128)} %param.15) | copy-start | bytes 18436
  13.6 169.6 %copy-start.4 = (f32[128,1]{0,1:T(1,128)}, f32[128,1]{0,1:T(1,128)S(1)}, u32[]{:S(2)}) copy-start(f32[128,1]{0,1:T(1,128)S(1)} %get-tuple-element.189) | copy-start | bytes 1540
  183.9 12.3 %collective-permute-start = (bf16[128,1536]{1,0:T(8,128)(2,1)S(1)}, bf16[128,1536]{1,0:T(8,128)(2,1)S(1)}, u32[]{:S(2)}, u32[]{:S(2)}) collective-permute-start(bf16[128,1536]{1,0:T(8,128)(2,1)S(1)} %get-tuple-element.98), channel_id=1, source_target_pairs={{64,0},{128,64},{192,128},{65,1},{129,65},{193,129},{66,2},{130,66... | collective-permute-start | bytes 1179656 | tf_op jit(solution)/shard_map/ppermute | solution.py:10
  196.2 11.4 %copy-start.2 = (f32[1536]{0:T(1024)}, f32[1536]{0:T(1024)S(1)}, u32[]{:S(2)}) copy-start(f32[1536]{0:T(1024)S(1)} %get-tuple-element.104) | copy-start | bytes 18436
  196.2 11.4 %collective-permute-start.1 = (bf16[128,1536]{1,0:T(8,128)(2,1)S(1)}, bf16[128,1536]{1,0:T(8,128)(2,1)S(1)}, u32[]{:S(2)}, u32[]{:S(2)}) collective-permute-start(bf16[128,1536]{1,0:T(8,128)(2,1)S(1)} %get-tuple-element.99), channel_id=1, source_target_pairs={{64,0},{128,64},{192,128},{65,1},{129,65},{193,129},{66,2},{130,66... | collective-permute-start | bytes 1179656 | tf_op jit(solution)/shard_map/ppermute | solution.py:10
  208.2 68.1 %collective-permute-start.2 = (bf16[128,1536]{1,0:T(8,128)(2,1)S(1)}, bf16[128,1536]{1,0:T(8,128)(2,1)S(1)}, u32[]{:S(2)}, u32[]{:S(2)}) collective-permute-start(bf16[128,1536]{1,0:T(8,128)(2,1)S(1)} %get-tuple-element.100), channel_id=1, source_target_pairs={{64,0},{128,64},{192,128},{65,1},{129,65},{193,129},{66,2},{130,66... | collective-permute-start | bytes 1179656 | tf_op jit(solution)/shard_map/ppermute | solution.py:10
  276.3 20.4 %copy-start.1 = (f32[1536]{0:T(1024)S(1)}, f32[1536]{0:T(1024)}, u32[]{:S(2)}) copy-start(f32[1536]{0:T(1024)} %get-tuple-element.105) | copy-start | bytes 18436
  276.3 20.4 %copy-start.3 = (f32[1536]{0:T(1024)S(1)}, f32[1536]{0:T(1024)}, u32[]{:S(2)}) copy-start(f32[1536]{0:T(1024)} %copy-done.2) | copy-start | bytes 18436
  282.5 12.7 %copy-start.7 = (f32[128,1]{0,1:T(1,128)S(1)}, f32[128,1]{0,1:T(1,128)}, u32[]{:S(2)}) copy-start(f32[128,1]{0,1:T(1,128)} %get-tuple-element.82) | copy-start | bytes 1540 | tf_op jit(solution)/shard_map/cond
Sparse Core Ops, SparseCore 0:
  10.7 88.3 all-gather.8
  101.8 81.3 all-gather.6
